TPU v7x, 256 devices: a whole 4x4x8 slice. The times are simulated.
256 devices in a mesh: seq: 128 (over y_hi, x, z, core), tp: 2 (over y_lo).
Axes of the slice: x: 4, y: 4 (y_hi: 2, y_lo: 2; y = y_hi * 2 + y_lo), z: 8, core: 2. Of those that a mesh axis runs over, the one named last changes fastest.
Arguments:
- noisy: bfloat16 [2, 49152, 1024], P(None, 'seq', 'tp'), may hold values from -6 to 6
- levels: int32 [2], replicated, may hold values from 0 to 999, as said below
- pairs: int32 [384, 4], P('seq'), may hold values from 0 to 383, as said below
- w_qkv: bfloat16 [3, 1024, 1024], P(None, None, 'tp'), may hold values from -4 to 4
- w_out: bfloat16 [1024, 1024], P('tp'), may hold values from -0.1875 to 0.1875
- w_up: bfloat16 [1024, 3072], P(None, 'tp'), may hold values from -0.1875 to 0.1875
- w_down: bfloat16 [3072, 1024], P('tp'), may hold values from -0.109375 to 0.109375
Outputs:
- denoised: bfloat16 [2, 49152, 1024], P(None, 'seq', 'tp')
Inputs may be any that keep to these rules, and one draw needn't show every extreme that they name: For query block b and section s, pairs[b, s] lies in the group of 3 consecutive blocks numbered g XOR (384 * 128 // (384 * 2 ** (s + 1))), where g = b // 3; at each section the query blocks of one group name each block of that group once. The samples' levels differ from one another; one sample has level 999.
All inputs are finite; a program needn't handle non-finite values.
Results may differ from a plain program's by a relative error of at most 0.017.
Values may be sent and summed in bfloat16 or wider, within the bound.
No kernel may reach another device: no remote copies, remote signals or barrier semaphores. Data moves between devices by JAX's collectives and lax.ppermute only.
A program may use at most 192 MiB of HBM per device.

v0:
```python
import functools
import math

import jax
import jax.numpy as jnp
from jax import lax
from jax.experimental import pallas as pl
from jax.experimental.pallas import tpu as pltpu
from jax.sharding import PartitionSpec as P


D = 1024
HEADS = 16
BLOCK = 128
SECTIONS = 4


def partner(x, axis, stride):
    return lax.ppermute(x, axis, [(i, i ^ 1 << stride) for i in range(lax.axis_size(axis))])


def tp_swap(x):
    return lax.ppermute(x, "tp", [(0, 1), (1, 0)])


def tp_join(own, other, tp_index):
    first = jnp.where(tp_index == 0, own, other)
    second = jnp.where(tp_index == 0, other, own)
    return jnp.concatenate([first, second], axis=-1)


def tp_half(x, index, width):
    return lax.dynamic_slice_in_dim(x, index * width, width, axis=x.ndim - 1)


def attention_kernel(off_ref, q_ref, kn_ref, vn_ref, *refs, head_dim):
    far_k = refs[0:2 * SECTIONS:2]
    far_v = refs[1:2 * SECTIONS:2]
    out_ref = refs[2 * SECTIONS]
    scale = 1.0 / math.sqrt(head_dim)
    dims = (((1,), (1,)), ((), ()))
    q = q_ref[0]
    tok_rows = q.shape[0]
    key_near = kn_ref[0, 0]
    value_near = vn_ref[0, 0]
    first = lax.broadcasted_iota(jnp.int32, q.shape, 1) < head_dim
    far_keys = []
    far_values = []
    for b in range(tok_rows // BLOCK):
        picks = [off_ref[b * SECTIONS + c] for c in range(SECTIONS)]
        far_keys.append(jnp.concatenate([far_k[c][0, 0, picks[c]] for c in range(SECTIONS)], axis=0))
        far_values.append(jnp.concatenate([far_v[c][0, 0, picks[c]] for c in range(SECTIONS)], axis=0))
    halves = []
    for own in (first, jnp.logical_not(first)):
        q_head = jnp.where(own, q, jnp.zeros_like(q))
        near_scores = lax.dot_general(q_head, key_near, dims, preferred_element_type=jnp.float32) * scale
        near_probs = []
        far_mixed = []
        for b in range(tok_rows // BLOCK):
            rows = slice(b * BLOCK, (b + 1) * BLOCK)
            near_b = near_scores[rows]
            far_b = lax.dot_general(
                q_head[rows], far_keys[b], dims, preferred_element_type=jnp.float32
            ) * scale
            top = jnp.maximum(near_b.max(axis=-1, keepdims=True), far_b.max(axis=-1, keepdims=True))
            near_e = jnp.exp(near_b - top)
            far_e = jnp.exp(far_b - top)
            total = near_e.sum(axis=-1, keepdims=True) + far_e.sum(axis=-1, keepdims=True)
            near_probs.append((near_e / total).astype(jnp.bfloat16))
            far_mixed.append(
                jnp.dot((far_e / total).astype(jnp.bfloat16), far_values[b],
                        preferred_element_type=jnp.float32)
            )
        mixed = jnp.dot(
            jnp.concatenate(near_probs, axis=0), value_near, preferred_element_type=jnp.float32
        ) + jnp.concatenate(far_mixed, axis=0)
        halves.append(mixed)
    out_ref[0] = jnp.where(first, halves[0], halves[1]).astype(out_ref.dtype)


def block_attention(queries, kv_here, got, offsets, head_dim):
    _, tok_rows, width = queries.shape
    blocks_dev = tok_rows // BLOCK
    lanes = 2 * head_dim
    in_specs = [
        pl.BlockSpec((1, tok_rows, lanes), lambda j, off: (0, 0, j)),
        pl.BlockSpec((1, 1, tok_rows, lanes), lambda j, off: (0, 0, 0, j)),
        pl.BlockSpec((1, 1, tok_rows, lanes), lambda j, off: (1, 0, 0, j)),
    ]
    operands = [queries, kv_here, kv_here]
    for section_idx in range(SECTIONS):
        for which in range(2):
            in_specs.append(
                pl.BlockSpec(
                    (1, 1, blocks_dev, BLOCK, lanes),
                    lambda j, off, w=which: (w, 0, 0, 0, j),
                )
            )
            operands.append(got[section_idx])
    grid_spec = pltpu.PrefetchScalarGridSpec(
        num_scalar_prefetch=1,
        grid=(width // lanes,),
        in_specs=in_specs,
        out_specs=pl.BlockSpec((1, tok_rows, lanes), lambda j, off: (0, 0, j)),
    )
    return pl.pallas_call(
        functools.partial(attention_kernel, head_dim=head_dim),
        grid_spec=grid_spec,
        out_shape=jax.ShapeDtypeStruct(queries.shape, queries.dtype),
    )(offsets, *operands)


def level_features(levels, model_width):
    half_count = model_width // 2
    index_row = jnp.arange(half_count, dtype=jnp.float32)
    freqs = jnp.exp(-math.log(10000.0) * index_row / half_count)
    angles = levels.astype(jnp.float32)[:, None] * freqs[None, :]
    return jnp.concatenate([jnp.sin(angles), jnp.cos(angles)], axis=1)


def rms_norm(values):
    return values * lax.rsqrt(jnp.mean(values * values, axis=-1, keepdims=True) + 1e-06)


def condition(gathered, level_feat):
    return (rms_norm(gathered.astype(jnp.float32)) + level_feat[:, None, :]).astype(jnp.bfloat16)


def per_device(noisy, levels, pairs, w_qkv, w_out, w_up, w_down):
    level_feat = level_features(levels, D)
    outs = []
    for s in range(noisy.shape[0]):
        outs.append(
            one_sample(noisy[s:s + 1], level_feat[s:s + 1], pairs, w_qkv, w_out, w_up, w_down)
        )
    return jnp.concatenate(outs, axis=0)


def one_sample(noisy, level_feat, pairs, w_qkv, w_out, w_up, w_down):
    samples, tok_rows, half_width = noisy.shape
    tp_index = lax.axis_index("tp")
    noisy_other = tp_swap(noisy)
    gathered = tp_join(noisy, noisy_other, tp_index)
    normed = condition(gathered, level_feat)
    projected = jnp.einsum(
        "std,cde->cste", normed, w_qkv, preferred_element_type=jnp.float32
    ).astype(jnp.bfloat16)
    queries, keys_here, values_here = (projected[0], projected[1], projected[2])
    blocks_dev = tok_rows // BLOCK
    head_dim = D // HEADS
    local_width = w_qkv.shape[2]
    axis_bits = lax.axis_size("seq").bit_length() - 1
    kv_here = jnp.stack([keys_here, values_here])
    offsets = (pairs % blocks_dev).astype(jnp.int32).reshape(-1)
    got = []
    for section_idx in range(SECTIONS):
        bit_pos = axis_bits - 1 - section_idx
        got.append(
            partner(kv_here, "seq", bit_pos).reshape(2, samples, blocks_dev, BLOCK, local_width)
        )
    mixed = block_attention(queries, kv_here, got, offsets, head_dim)
    outs = []
    for chunk in range(blocks_dev):
        rows = slice(chunk * BLOCK, (chunk + 1) * BLOCK)
        outs.append(
            finish_rows(mixed[:, rows], gathered[:, rows], tp_index, half_width, w_out, w_up, w_down)
        )
    return jnp.concatenate(outs, axis=1)


def finish_rows(mixed, gathered, tp_index, half_width, w_out, w_up, w_down):
    attn_part = jnp.einsum("sth,hd->std", mixed, w_out, preferred_element_type=jnp.float32)
    attn_own = attn_part.astype(jnp.bfloat16)
    attn_other = tp_swap(attn_own)
    attn_sum = attn_own.astype(jnp.float32) + attn_other.astype(jnp.float32)
    middle = (gathered.astype(jnp.float32) + attn_sum).astype(jnp.bfloat16)
    middle_half = tp_half(middle, tp_index, half_width)
    inner = rms_norm(middle.astype(jnp.float32)).astype(jnp.bfloat16)
    hidden = jax.nn.gelu(
        jnp.einsum("std,df->stf", inner, w_up, preferred_element_type=jnp.float32), approximate=True
    ).astype(jnp.bfloat16)
    down_part = jnp.einsum("stf,fd->std", hidden, w_down, preferred_element_type=jnp.float32)
    down_own = tp_half(down_part, tp_index, half_width)
    down_send = tp_half(down_part, 1 - tp_index, half_width).astype(jnp.bfloat16)
    down_half = down_own + tp_swap(down_send).astype(jnp.float32)
    return (middle_half.astype(jnp.float32) + down_half).astype(jnp.bfloat16)


def solution(mesh):
    in_specs = (
        P(None, "seq", "tp"),
        P(),
        P("seq", None),
        P(None, None, "tp"),
        P("tp", None),
        P(None, "tp"),
        P("tp", None),
    )
    out_specs = P(None, "seq", "tp")
    return jax.shard_map(
        per_device, mesh=mesh, in_specs=in_specs, out_specs=out_specs, check_vma=False
    )
```

profile of v0, /device:TPU:2, one launch (start us, length us, event | category | flops | bytes accessed | tf_op | source)
XLA Modules:
  0.0 191.5 jit_solution(13572078699499999439)
XLA Ops:
  3.7 8.5 %collective-permute-done = bf16[1,384,512]{2,1,0:T(8,128)(2,1)} collective-permute-done((bf16[1,384,512]{2,1,0:T(8,128)(2,1)S(1)}, bf16[1,384,512]{2,1,0:T(8,128)(2,1)}, u32[]{:S(2)}, u32[]{:S(2)}) %collective-permute-start) | collective-permute-done | bytes 393248 | tf_op jit(solution)/shard_map/ppermute | solution.py:23
  12.2 2.1 %broadcast_select_fusion.3 = (bf16[1,384,512]{2,1,0:T(8,128)(2,1)S(1)}, bf16[1,384,512]{2,1,0:T(8,128)(2,1)S(1)}, bf16[1,384,512]{2,1,0:T(8,128)(2,1)}) fusion(bf16[1,384,512]{2,1,0:T(8,128)(2,1)} %collective-permute-done, pred[]{:T(512)S(6)} %eq.5, bf16[2,384,512]{2,1,0:T(8,128)(2,1)} %param.7), kind=kLoop, calls=%fused_computation.166 | loop fusion | flops 393216 | bytes 2359297 | tf_op jit(solution)/shard_map/jit(_where)/select_n | solution.py:27
  17.3 3.2 %collective-permute-start.1 = (bf16[2,1,384,512]{3,2,1,0:T(8,128)(2,1)}, bf16[2,1,384,512]{3,2,1,0:T(8,128)(2,1)}, u32[]{:S(2)}, u32[]{:S(2)}) collective-permute-start(bf16[2,1,384,512]{3,2,1,0:T(8,128)(2,1)} %stack.8.kn_ref.vn_ref), channel_id=1, source_target_pairs={{0,128},{2,130},{4,132},{6,134},{8,136},{10,138},{12,140},{14,142}... | collective-permute-start | bytes 2359304 | tf_op jit(solution)/shard_map/ppermute | solution.py:19
  20.5 2.1 %collective-permute-start.2 = (bf16[2,1,384,512]{3,2,1,0:T(8,128)(2,1)}, bf16[2,1,384,512]{3,2,1,0:T(8,128)(2,1)}, u32[]{:S(2)}, u32[]{:S(2)}) collective-permute-start(bf16[2,1,384,512]{3,2,1,0:T(8,128)(2,1)} %stack.8.kn_ref.vn_ref), channel_id=1, source_target_pairs={{0,64},{2,66},{4,68},{6,70},{8,72},{10,74},{12,76},{14,78},{16,80}... | collective-permute-start | bytes 2359304 | tf_op jit(solution)/shard_map/ppermute | solution.py:19
  24.1 7.2 %collective-permute-start.4 = (bf16[2,1,384,512]{3,2,1,0:T(8,128)(2,1)}, bf16[2,1,384,512]{3,2,1,0:T(8,128)(2,1)}, u32[]{:S(2)}, u32[]{:S(2)}) collective-permute-start(bf16[2,1,384,512]{3,2,1,0:T(8,128)(2,1)} %stack.8.kn_ref.vn_ref), channel_id=1, source_target_pairs={{0,16},{2,18},{4,20},{6,22},{8,24},{10,26},{12,28},{14,30},{16,0},... | collective-permute-start | bytes 2359304 | tf_op jit(solution)/shard_map/ppermute | solution.py:19
  32.6 1.8 slice_bitcast_fusion.1.q_ref
  34.4 12.0 %collective-permute-done.11 = bf16[1,384,512]{2,1,0:T(8,128)(2,1)} collective-permute-done((bf16[1,384,512]{2,1,0:T(8,128)(2,1)}, bf16[1,384,512]{2,1,0:T(8,128)(2,1)}, u32[]{:S(2)}, u32[]{:S(2)}) %collective-permute-start.11) | collective-permute-done | bytes 393248 | tf_op jit(solution)/shard_map/ppermute | solution.py:23
  48.6 8.8 %collective-permute-done.3 = bf16[2,1,384,512]{3,2,1,0:T(8,128)(2,1)} collective-permute-done((bf16[2,1,384,512]{3,2,1,0:T(8,128)(2,1)}, bf16[2,1,384,512]{3,2,1,0:T(8,128)(2,1)}, u32[]{:S(2)}, u32[]{:S(2)}) %collective-permute-start.3) | collective-permute-done | bytes 786464 | tf_op jit(solution)/shard_map/ppermute | solution.py:19
  57.4 5.6 %collective-permute-done.4 = bf16[2,1,384,512]{3,2,1,0:T(8,128)(2,1)} collective-permute-done((bf16[2,1,384,512]{3,2,1,0:T(8,128)(2,1)}, bf16[2,1,384,512]{3,2,1,0:T(8,128)(2,1)}, u32[]{:S(2)}, u32[]{:S(2)}) %collective-permute-start.4) | collective-permute-done | bytes 786464 | tf_op jit(solution)/shard_map/ppermute | solution.py:19
  62.9 13.8 %shard_map.73 = bf16[1,384,512]{2,1,0:T(8,128)(2,1)} custom-call(s32[12]{0:T(128)} %reshape.430.off_ref, bf16[1,384,512]{2,1,0:T(8,128)(2,1)} %slice_bitcast_fusion.1.q_ref, bf16[2,1,384,512]{3,2,1,0:T(8,128)(2,1)} %stack.8.kn_ref.vn_ref, bf16[2,1,384,512]{3,2,1,0:T(8,128)(2,1)} %stack.8.kn_ref.vn_ref, bf16[2,1,3,128,512]{4,3,2,1,0:T(8,128)(2,1)} %bitcast.10.refs_0_.refs_1_, ...), custom_call_target="tpu_custom_call" | custom-call | tf_op jit(solution)/shard_map/pallas_call | solution.py:106
  86.6 1.8 collective-permute-start.12
  91.8 4.5 %collective-permute-done.7 = bf16[1,128,1024]{2,1,0:T(8,128)(2,1)S(1)} collective-permute-done((bf16[1,128,1024]{2,1,0:T(8,128)(2,1)S(1)}, bf16[1,128,1024]{2,1,0:T(8,128)(2,1)S(1)}, u32[]{:S(2)}, u32[]{:S(2)}) %collective-permute-start.7) | collective-permute-done | bytes 262176 | tf_op jit(solution)/shard_map/ppermute | solution.py:23
  96.2 6.4 %collective-permute-start.15 = (bf16[2,1,384,512]{3,2,1,0:T(8,128)(2,1)}, bf16[2,1,384,512]{3,2,1,0:T(8,128)(2,1)}, u32[]{:S(2)}, u32[]{:S(2)}) collective-permute-start(bf16[2,1,384,512]{3,2,1,0:T(8,128)(2,1)} %stack.9.kn_ref.vn_ref), channel_id=1, source_target_pairs={{0,16},{2,18},{4,20},{6,22},{8,24},{10,26},{12,28},{14,30},{16,0},... | collective-permute-start | bytes 2359304 | tf_op jit(solution)/shard_map/ppermute | solution.py:19
  103.8 5.0 %fusion.88 = f32[128,1024]{1,0:T(8,128)} fusion(bf16[1536,1024]{1,0:T(8,128)(2,1)} %param.13, bf16[1024,1536]{1,0:T(8,128)(2,1)} %param.12, bf16[1,128,1024]{2,1,0:T(8,128)(2,1)} %get-tuple-element.24, f32[128]{0:T(128)S(1)} %add_rsqrt_fusion.5), kind=kOutput, calls=%fused_computation.134 | convolution fusion | flops 807469056 | bytes 7078400 | tf_op jit(solution)/shard_map/stf,fd->std/dot_general | solution.py:182
  110.6 5.0 %fusion.90 = f32[128,1024]{1,0:T(8,128)} fusion(bf16[1536,1024]{1,0:T(8,128)(2,1)} %param.13, bf16[1024,1536]{1,0:T(8,128)(2,1)} %param.12, bf16[1,128,1024]{2,1,0:T(8,128)(2,1)} %get-tuple-element.22, f32[128]{0:T(128)S(1)} %add_rsqrt_fusion.6), kind=kOutput, calls=%fused_computation.135 | convolution fusion | flops 807469056 | bytes 7078400 | tf_op jit(solution)/shard_map/stf,fd->std/dot_general | solution.py:182
  117.2 4.9 %fusion.92 = f32[128,1024]{1,0:T(8,128)} fusion(bf16[1536,1024]{1,0:T(8,128)(2,1)} %param.13, bf16[1024,1536]{1,0:T(8,128)(2,1)} %param.12, bf16[1,128,1024]{2,1,0:T(8,128)(2,1)S(1)} %copy-done.12, f32[128]{0:T(128)S(1)} %add_rsqrt_fusion.7), kind=kOutput, calls=%fused_computation.136 | convolution fusion | flops 807469056 | bytes 7078400 | tf_op jit(solution)/shard_map/stf,fd->std/dot_general | solution.py:182
  125.7 4.1 %collective-permute-done.15 = bf16[2,1,384,512]{3,2,1,0:T(8,128)(2,1)} collective-permute-done((bf16[2,1,384,512]{3,2,1,0:T(8,128)(2,1)}, bf16[2,1,384,512]{3,2,1,0:T(8,128)(2,1)}, u32[]{:S(2)}, u32[]{:S(2)}) %collective-permute-start.15) | collective-permute-done | bytes 786464 | tf_op jit(solution)/shard_map/ppermute | solution.py:19
  129.8 13.8 %shard_map.74 = bf16[1,384,512]{2,1,0:T(8,128)(2,1)} custom-call(s32[12]{0:T(128)} %reshape.430.off_ref, bf16[1,384,512]{2,1,0:T(8,128)(2,1)} %slice_bitcast_fusion.q_ref, bf16[2,1,384,512]{3,2,1,0:T(8,128)(2,1)} %stack.9.kn_ref.vn_ref, bf16[2,1,384,512]{3,2,1,0:T(8,128)(2,1)} %stack.9.kn_ref.vn_ref, bf16[2,1,3,128,512]{4,3,2,1,0:T(8,128)(2,1)} %bitcast.39.refs_0_.refs_1_, ...), custom_call_target="tpu_custom_call" | custom-call | tf_op jit(solution)/shard_map/pallas_call | solution.py:106
  143.7 1.7 fusion.5
  157.1 4.2 %collective-permute-done.20 = bf16[1,128,1024]{2,1,0:T(8,128)(2,1)S(1)} collective-permute-done((bf16[1,128,1024]{2,1,0:T(8,128)(2,1)S(1)}, bf16[1,128,1024]{2,1,0:T(8,128)(2,1)S(1)}, u32[]{:S(2)}, u32[]{:S(2)}) %collective-permute-start.20) | collective-permute-done | bytes 262176 | tf_op jit(solution)/shard_map/ppermute | solution.py:23
  162.5 5.0 %fusion.82 = f32[128,1024]{1,0:T(8,128)} fusion(bf16[1536,1024]{1,0:T(8,128)(2,1)} %param.13, bf16[1024,1536]{1,0:T(8,128)(2,1)} %param.12, bf16[1,128,1024]{2,1,0:T(8,128)(2,1)} %get-tuple-element.29, f32[128]{0:T(128)S(1)} %add_rsqrt_fusion.2), kind=kOutput, calls=%fused_computation.131 | convolution fusion | flops 807469056 | bytes 7078400 | tf_op jit(solution)/shard_map/stf,fd->std/dot_general | solution.py:182
  170.4 5.0 %fusion.84 = f32[128,1024]{1,0:T(8,128)} fusion(bf16[1536,1024]{1,0:T(8,128)(2,1)} %param.13, bf16[1024,1536]{1,0:T(8,128)(2,1)} %param.12, bf16[1,128,1024]{2,1,0:T(8,128)(2,1)} %get-tuple-element.27, f32[128]{0:T(128)S(1)} %add_rsqrt_fusion.3), kind=kOutput, calls=%fused_computation.132 | convolution fusion | flops 807469056 | bytes 7078400 | tf_op jit(solution)/shard_map/stf,fd->std/dot_general | solution.py:182
  177.7 4.9 %fusion.86 = f32[128,1024]{1,0:T(8,128)} fusion(bf16[1536,1024]{1,0:T(8,128)(2,1)} %param.13, bf16[1024,1536]{1,0:T(8,128)(2,1)} %param.12, bf16[1,128,1024]{2,1,0:T(8,128)(2,1)S(1)} %get-tuple-element.12, f32[128]{0:T(128)S(1)} %add_rsqrt_fusion.4), kind=kOutput, calls=%fused_computation.133 | convolution fusion | flops 807469056 | bytes 7078400 | tf_op jit(solution)/shard_map/stf,fd->std/dot_general | solution.py:182
  189.6 1.9 maximum_maximum_fusion
  (112 shorter events, 57.9 us)
Async XLA Ops:
  1.2 11.0 %collective-permute-start = (bf16[1,384,512]{2,1,0:T(8,128)(2,1)S(1)}, bf16[1,384,512]{2,1,0:T(8,128)(2,1)}, u32[]{:S(2)}, u32[]{:S(2)}) collective-permute-start(bf16[1,384,512]{2,1,0:T(8,128)(2,1)S(1)} %slice.64), channel_id=1, source_target_pairs={{0,1},{1,0},{2,3},{3,2},{4,5},{5,4},{6,7},{7,6},{8,9},{9,8},{10,11... | collective-permute-start | bytes 1179656 | tf_op jit(solution)/shard_map/ppermute | solution.py:23
  17.3 31.2 %collective-permute-start.1 = (bf16[2,1,384,512]{3,2,1,0:T(8,128)(2,1)}, bf16[2,1,384,512]{3,2,1,0:T(8,128)(2,1)}, u32[]{:S(2)}, u32[]{:S(2)}) collective-permute-start(bf16[2,1,384,512]{3,2,1,0:T(8,128)(2,1)} %stack.8.kn_ref.vn_ref), channel_id=1, source_target_pairs={{0,128},{2,130},{4,132},{6,134},{8,136},{10,138},{12,140},{14,142}... | collective-permute-start | bytes 2359304 | tf_op jit(solution)/shard_map/ppermute | solution.py:19
  20.5 28.0 %collective-permute-start.2 = (bf16[2,1,384,512]{3,2,1,0:T(8,128)(2,1)}, bf16[2,1,384,512]{3,2,1,0:T(8,128)(2,1)}, u32[]{:S(2)}, u32[]{:S(2)}) collective-permute-start(bf16[2,1,384,512]{3,2,1,0:T(8,128)(2,1)} %stack.8.kn_ref.vn_ref), channel_id=1, source_target_pairs={{0,64},{2,66},{4,68},{6,70},{8,72},{10,74},{12,76},{14,78},{16,80}... | collective-permute-start | bytes 2359304 | tf_op jit(solution)/shard_map/ppermute | solution.py:19
  22.7 34.7 %collective-permute-start.3 = (bf16[2,1,384,512]{3,2,1,0:T(8,128)(2,1)}, bf16[2,1,384,512]{3,2,1,0:T(8,128)(2,1)}, u32[]{:S(2)}, u32[]{:S(2)}) collective-permute-start(bf16[2,1,384,512]{3,2,1,0:T(8,128)(2,1)} %stack.8.kn_ref.vn_ref), channel_id=1, source_target_pairs={{0,32},{2,34},{4,36},{6,38},{8,40},{10,42},{12,44},{14,46},{16,48}... | collective-permute-start | bytes 2359304 | tf_op jit(solution)/shard_map/ppermute | solution.py:19
  24.1 38.9 %collective-permute-start.4 = (bf16[2,1,384,512]{3,2,1,0:T(8,128)(2,1)}, bf16[2,1,384,512]{3,2,1,0:T(8,128)(2,1)}, u32[]{:S(2)}, u32[]{:S(2)}) collective-permute-start(bf16[2,1,384,512]{3,2,1,0:T(8,128)(2,1)} %stack.8.kn_ref.vn_ref), channel_id=1, source_target_pairs={{0,16},{2,18},{4,20},{6,22},{8,24},{10,26},{12,28},{14,30},{16,0},... | collective-permute-start | bytes 2359304 | tf_op jit(solution)/shard_map/ppermute | solution.py:19
  31.3 15.1 %collective-permute-start.11 = (bf16[1,384,512]{2,1,0:T(8,128)(2,1)}, bf16[1,384,512]{2,1,0:T(8,128)(2,1)}, u32[]{:S(2)}, u32[]{:S(2)}) collective-permute-start(bf16[1,384,512]{2,1,0:T(8,128)(2,1)} %get-tuple-element.25), channel_id=1, source_target_pairs={{0,1},{1,0},{2,3},{3,2},{4,5},{5,4},{6,7},{7,6},{8,9},{9,8},{10,11... | collective-permute-start | bytes 1179656 | tf_op jit(solution)/shard_map/ppermute | solution.py:23
  81.4 9.3 %collective-permute-start.5 = (bf16[1,128,1024]{2,1,0:T(8,128)(2,1)S(1)}, bf16[1,128,1024]{2,1,0:T(8,128)(2,1)S(1)}, u32[]{:S(2)}, u32[]{:S(2)}) collective-permute-start(bf16[1,128,1024]{2,1,0:T(8,128)(2,1)S(1)} %fusion.2), channel_id=1, source_target_pairs={{0,1},{1,0},{2,3},{3,2},{4,5},{5,4},{6,7},{7,6},{8,9},{9,8},{10,11... | collective-permute-start | bytes 786440 | tf_op jit(solution)/shard_map/ppermute | solution.py:23
  82.1 14.1 %collective-permute-start.7 = (bf16[1,128,1024]{2,1,0:T(8,128)(2,1)S(1)}, bf16[1,128,1024]{2,1,0:T(8,128)(2,1)S(1)}, u32[]{:S(2)}, u32[]{:S(2)}) collective-permute-start(bf16[1,128,1024]{2,1,0:T(8,128)(2,1)S(1)} %fusion.3), channel_id=1, source_target_pairs={{0,1},{1,0},{2,3},{3,2},{4,5},{5,4},{6,7},{7,6},{8,9},{9,8},{10,11... | collective-permute-start | bytes 786440 | tf_op jit(solution)/shard_map/ppermute | solution.py:23
  83.5 19.2 %collective-permute-start.9 = (bf16[1,128,1024]{2,1,0:T(8,128)(2,1)S(1)}, bf16[1,128,1024]{2,1,0:T(8,128)(2,1)S(1)}, u32[]{:S(2)}, u32[]{:S(2)}) collective-permute-start(bf16[1,128,1024]{2,1,0:T(8,128)(2,1)S(1)} %fusion.4), channel_id=1, source_target_pairs={{0,1},{1,0},{2,3},{3,2},{4,5},{5,4},{6,7},{7,6},{8,9},{9,8},{10,11... | collective-permute-start | bytes 786440 | tf_op jit(solution)/shard_map/ppermute | solution.py:23
  84.2 18.5 %copy-start.4 = (bf16[1,384,512]{2,1,0:T(8,128)(2,1)S(1)}, bf16[1,384,512]{2,1,0:T(8,128)(2,1)}, u32[]{:S(2)}) copy-start(bf16[1,384,512]{2,1,0:T(8,128)(2,1)} %copy-done.3) | copy-start | bytes 1179652
  86.6 37.2 %collective-permute-start.12 = (bf16[2,1,384,512]{3,2,1,0:T(8,128)(2,1)}, bf16[2,1,384,512]{3,2,1,0:T(8,128)(2,1)}, u32[]{:S(2)}, u32[]{:S(2)}) collective-permute-start(bf16[2,1,384,512]{3,2,1,0:T(8,128)(2,1)} %stack.9.kn_ref.vn_ref), channel_id=1, source_target_pairs={{0,128},{2,130},{4,132},{6,134},{8,136},{10,138},{12,140},{14,142}... | collective-permute-start | bytes 2359304 | tf_op jit(solution)/shard_map/ppermute | solution.py:19
  88.4 36.7 %collective-permute-start.13 = (bf16[2,1,384,512]{3,2,1,0:T(8,128)(2,1)}, bf16[2,1,384,512]{3,2,1,0:T(8,128)(2,1)}, u32[]{:S(2)}, u32[]{:S(2)}) collective-permute-start(bf16[2,1,384,512]{3,2,1,0:T(8,128)(2,1)} %stack.9.kn_ref.vn_ref), channel_id=1, source_target_pairs={{0,64},{2,66},{4,68},{6,70},{8,72},{10,74},{12,76},{14,78},{16,80}... | collective-permute-start | bytes 2359304 | tf_op jit(solution)/shard_map/ppermute | solution.py:19
  90.6 35.1 %collective-permute-start.14 = (bf16[2,1,384,512]{3,2,1,0:T(8,128)(2,1)}, bf16[2,1,384,512]{3,2,1,0:T(8,128)(2,1)}, u32[]{:S(2)}, u32[]{:S(2)}) collective-permute-start(bf16[2,1,384,512]{3,2,1,0:T(8,128)(2,1)} %stack.9.kn_ref.vn_ref), channel_id=1, source_target_pairs={{0,32},{2,34},{4,36},{6,38},{8,40},{10,42},{12,44},{14,46},{16,48}... | collective-permute-start | bytes 2359304 | tf_op jit(solution)/shard_map/ppermute | solution.py:19
  96.2 33.5 %collective-permute-start.15 = (bf16[2,1,384,512]{3,2,1,0:T(8,128)(2,1)}, bf16[2,1,384,512]{3,2,1,0:T(8,128)(2,1)}, u32[]{:S(2)}, u32[]{:S(2)}) collective-permute-start(bf16[2,1,384,512]{3,2,1,0:T(8,128)(2,1)} %stack.9.kn_ref.vn_ref), channel_id=1, source_target_pairs={{0,16},{2,18},{4,20},{6,22},{8,24},{10,26},{12,28},{14,30},{16,0},... | collective-permute-start | bytes 2359304 | tf_op jit(solution)/shard_map/ppermute | solution.py:19
  109.8 40.6 %collective-permute-start.10 = (bf16[1,128,512]{2,1,0:T(8,128)(2,1)S(1)}, bf16[1,128,512]{2,1,0:T(8,128)(2,1)}, u32[]{:S(2)}, u32[]{:S(2)}) collective-permute-start(bf16[1,128,512]{2,1,0:T(8,128)(2,1)S(1)} %fusion.192), channel_id=1, source_target_pairs={{0,1},{1,0},{2,3},{3,2},{4,5},{5,4},{6,7},{7,6},{8,9},{9,8},{10,11... | collective-permute-start | bytes 393224 | tf_op jit(solution)/shard_map/ppermute | solution.py:23
  123.7 28.7 %collective-permute-start.8 = (bf16[1,128,512]{2,1,0:T(8,128)(2,1)}, bf16[1,128,512]{2,1,0:T(8,128)(2,1)}, u32[]{:S(2)}, u32[]{:S(2)}) collective-permute-start(bf16[1,128,512]{2,1,0:T(8,128)(2,1)} %fusion.191), channel_id=1, source_target_pairs={{0,1},{1,0},{2,3},{3,2},{4,5},{5,4},{6,7},{7,6},{8,9},{9,8},{10,11... | collective-permute-start | bytes 393224 | tf_op jit(solution)/shard_map/ppermute | solution.py:23
  125.1 29.0 %collective-permute-start.6 = (bf16[1,128,512]{2,1,0:T(8,128)(2,1)}, bf16[1,128,512]{2,1,0:T(8,128)(2,1)}, u32[]{:S(2)}, u32[]{:S(2)}) collective-permute-start(bf16[1,128,512]{2,1,0:T(8,128)(2,1)} %fusion.190), channel_id=1, source_target_pairs={{0,1},{1,0},{2,3},{3,2},{4,5},{5,4},{6,7},{7,6},{8,9},{9,8},{10,11... | collective-permute-start | bytes 393224 | tf_op jit(solution)/shard_map/ppermute | solution.py:23
  143.7 17.6 %copy-start.7 = (bf16[1,384,512]{2,1,0:T(8,128)(2,1)S(1)}, bf16[1,384,512]{2,1,0:T(8,128)(2,1)}, u32[]{:S(2)}) copy-start(bf16[1,384,512]{2,1,0:T(8,128)(2,1)} %copy-done.5) | copy-start | bytes 1179652
  147.1 8.5 %collective-permute-start.16 = (bf16[1,128,1024]{2,1,0:T(8,128)(2,1)S(1)}, bf16[1,128,1024]{2,1,0:T(8,128)(2,1)S(1)}, u32[]{:S(2)}, u32[]{:S(2)}) collective-permute-start(bf16[1,128,1024]{2,1,0:T(8,128)(2,1)S(1)} %fusion.5), channel_id=1, source_target_pairs={{0,1},{1,0},{2,3},{3,2},{4,5},{5,4},{6,7},{7,6},{8,9},{9,8},{10,11... | collective-permute-start | bytes 786440 | tf_op jit(solution)/shard_map/ppermute | solution.py:23
  147.8 9.2 %collective-permute-start.18 = (bf16[1,128,1024]{2,1,0:T(8,128)(2,1)S(1)}, bf16[1,128,1024]{2,1,0:T(8,128)(2,1)S(1)}, u32[]{:S(2)}, u32[]{:S(2)}) collective-permute-start(bf16[1,128,1024]{2,1,0:T(8,128)(2,1)S(1)} %fusion.6), channel_id=1, source_target_pairs={{0,1},{1,0},{2,3},{3,2},{4,5},{5,4},{6,7},{7,6},{8,9},{9,8},{10,11... | collective-permute-start | bytes 786440 | tf_op jit(solution)/shard_map/ppermute | solution.py:23
  150.4 10.8 %collective-permute-start.20 = (bf16[1,128,1024]{2,1,0:T(8,128)(2,1)S(1)}, bf16[1,128,1024]{2,1,0:T(8,128)(2,1)S(1)}, u32[]{:S(2)}, u32[]{:S(2)}) collective-permute-start(bf16[1,128,1024]{2,1,0:T(8,128)(2,1)S(1)} %fusion.7), channel_id=1, source_target_pairs={{0,1},{1,0},{2,3},{3,2},{4,5},{5,4},{6,7},{7,6},{8,9},{9,8},{10,11... | collective-permute-start | bytes 786440 | tf_op jit(solution)/shard_map/ppermute | solution.py:23
  169.1 16.0 %collective-permute-start.21 = (bf16[1,128,512]{2,1,0:T(8,128)(2,1)}, bf16[1,128,512]{2,1,0:T(8,128)(2,1)}, u32[]{:S(2)}, u32[]{:S(2)}) collective-permute-start(bf16[1,128,512]{2,1,0:T(8,128)(2,1)} %fusion.195), channel_id=1, source_target_pairs={{0,1},{1,0},{2,3},{3,2},{4,5},{5,4},{6,7},{7,6},{8,9},{9,8},{10,11... | collective-permute-start | bytes 393224 | tf_op jit(solution)/shard_map/ppermute | solution.py:23
  177.0 9.1 %collective-permute-start.19 = (bf16[1,128,512]{2,1,0:T(8,128)(2,1)}, bf16[1,128,512]{2,1,0:T(8,128)(2,1)}, u32[]{:S(2)}, u32[]{:S(2)}) collective-permute-start(bf16[1,128,512]{2,1,0:T(8,128)(2,1)} %fusion.194), channel_id=1, source_target_pairs={{0,1},{1,0},{2,3},{3,2},{4,5},{5,4},{6,7},{7,6},{8,9},{9,8},{10,11... | collective-permute-start | bytes 393224 | tf_op jit(solution)/shard_map/ppermute | solution.py:23
  183.6 5.1 %collective-permute-start.17 = (bf16[1,128,512]{2,1,0:T(8,128)(2,1)S(1)}, bf16[1,128,512]{2,1,0:T(8,128)(2,1)S(1)}, u32[]{:S(2)}, u32[]{:S(2)}) collective-permute-start(bf16[1,128,512]{2,1,0:T(8,128)(2,1)S(1)} %fusion.193), channel_id=1, source_target_pairs={{0,1},{1,0},{2,3},{3,2},{4,5},{5,4},{6,7},{7,6},{8,9},{9,8},{10,11... | collective-permute-start | bytes 393224 | tf_op jit(solution)/shard_map/ppermute | solution.py:23
  (17 other events, 128.1 us)
where the time goes:
time: 192 us
  waiting for transfers between devices  51.7 us (27%)
  matrix products  41.8 us (22%)
  starting transfers between devices  38 us (20%)
  Pallas kernels  27.6 us (14%)
  other arithmetic  16.2 us (8%)
  local copies, waits for them, and re-layouts  15.8 us (8%)
    ppermute x14, waiting for transfers between devices, tp_swap(): return lax.ppermute(x, 'tp', [(0, 1), (1, 0)])  33.3 us
    dot_general x6, matrix products, finish_rows(): jnp.einsum('stf,fd->std', hidden, w_down, preferred_element_type=jnp.floa...  29.7 us
    pallas_call x2, Pallas kernels, block_attention(): pl.pallas_call(functools.partial(attention_kernel, head_dim=head_dim), gr...  27.6 us
    ppermute x8, starting transfers between devices, partner(): lax.ppermute(x, axis, [(i, i ^ 1 << stride) for i in range(lax.axis_size(...  23.5 us
    ppermute x8, waiting for transfers between devices, partner(): lax.ppermute(x, axis, [(i, i ^ 1 << stride) for i in range(lax.axis_size(...  18.4 us
    ppermute x14, starting transfers between devices, tp_swap(): return lax.ppermute(x, 'tp', [(0, 1), (1, 0)])  14.5 us
    dot_general x6, matrix products, finish_rows(): jnp.einsum('sth,hd->std', mixed, w_out, preferred_element_type=jnp.float32)  9.13 us
    convert_element_type x6, local copies, waits for them, and re-layouts, finish_rows(): tp_half(down_part, 1 - tp_index, half_width).astype(jnp.bfloat16)  8.39 us
  transfers between devices with their start and end apart: 22, of which 10 were waited for; matrix products, arithmetic and copies ran while one was open for 27% of the time, Pallas kernels for 7%

commit v1 on v0

--- a/solution.py
+++ b/solution.py
@@ -159,16 +159,6 @@
             partner(kv_here, "seq", bit_pos).reshape(2, samples, blocks_dev, BLOCK, local_width)
         )
     mixed = block_attention(queries, kv_here, got, offsets, head_dim)
-    outs = []
-    for chunk in range(blocks_dev):
-        rows = slice(chunk * BLOCK, (chunk + 1) * BLOCK)
-        outs.append(
-            finish_rows(mixed[:, rows], gathered[:, rows], tp_index, half_width, w_out, w_up, w_down)
-        )
-    return jnp.concatenate(outs, axis=1)
-
-
-def finish_rows(mixed, gathered, tp_index, half_width, w_out, w_up, w_down):
     attn_part = jnp.einsum("sth,hd->std", mixed, w_out, preferred_element_type=jnp.float32)
     attn_own = attn_part.astype(jnp.bfloat16)
     attn_other = tp_swap(attn_own)
@@ -177,7 +167,8 @@
     middle_half = tp_half(middle, tp_index, half_width)
     inner = rms_norm(middle.astype(jnp.float32)).astype(jnp.bfloat16)
     hidden = jax.nn.gelu(
-        jnp.einsum("std,df->stf", inner, w_up, preferred_element_type=jnp.float32), approximate=True
+        jnp.einsum("std,df->stf", inner, w_up, preferred_element_type=jnp.float32),
+        approximate=True,
     ).astype(jnp.bfloat16)
     down_part = jnp.einsum("stf,fd->std", hidden, w_down, preferred_element_type=jnp.float32)
     down_own = tp_half(down_part, tp_index, half_width)

time: 192 us -> 162 us (0.84)
  the two profiles are of different devices: /device:TPU:2 before, /device:TPU:1 now
where the time goes in v1:
time: 162 us; the launch traced here: 160 us
  waiting for transfers between devices  57.5 us (35%)
  starting transfers between devices  29.3 us (18%)
  Pallas kernels  27.6 us (17%)
  matrix products  22.7 us (14%)
  other arithmetic  12.7 us (8%)
  local copies, waits for them, and re-layouts  10.2 us (6%)
    ppermute x8, waiting for transfers between devices, partner(): lax.ppermute(x, axis, [(i, i ^ 1 << stride) for i in range(lax.axis_size(...  39.3 us
    pallas_call x2, Pallas kernels, block_attention(): pl.pallas_call(functools.partial(attention_kernel, head_dim=head_dim), gr...  27.6 us
    ppermute x8, starting transfers between devices, partner(): lax.ppermute(x, axis, [(i, i ^ 1 << stride) for i in range(lax.axis_size(...  23.1 us
    ppermute x6, waiting for transfers between devices, tp_swap(): return lax.ppermute(x, 'tp', [(0, 1), (1, 0)])  18.3 us
    dot_general x2, matrix products, one_sample(): jnp.einsum('stf,fd->std', hidden, w_down, preferred_element_type=jnp.floa...  14.1 us
    ppermute x6, starting transfers between devices, tp_swap(): return lax.ppermute(x, 'tp', [(0, 1), (1, 0)])  6.21 us
    reduce_sum x4, other arithmetic, rms_norm(): jnp.mean(values * values, axis=-1, keepdims=True) + 1e-06  5.84 us
    dot_general x2, matrix products, one_sample(): jnp.einsum('sth,hd->std', mixed, w_out, preferred_element_type=jnp.float32)  5.67 us
  transfers between devices with their start and end apart: 14, of which 7 were waited for; matrix products, arithmetic and copies ran while one was open for 25% of the time, Pallas kernels for 17%

profile of v1, /device:TPU:1, one launch (start us, length us, event | category | flops | bytes accessed | tf_op | source)
XLA Modules:
  0.0 160.3 jit_solution(7718405239147717492)
XLA Ops:
  1.2 2.2 %collective-permute-start = (bf16[1,384,512]{2,1,0:T(8,128)(2,1)S(1)}, bf16[1,384,512]{2,1,0:T(8,128)(2,1)}, u32[]{:S(2)}, u32[]{:S(2)}) collective-permute-start(bf16[1,384,512]{2,1,0:T(8,128)(2,1)S(1)} %slice.28), channel_id=1, source_target_pairs={{0,1},{1,0},{2,3},{3,2},{4,5},{5,4},{6,7},{7,6},{8,9},{9,8},{10,11... | collective-permute-start | bytes 1179656 | tf_op jit(solution)/shard_map/ppermute | solution.py:23
  5.5 5.5 %collective-permute-done = bf16[1,384,512]{2,1,0:T(8,128)(2,1)} collective-permute-done((bf16[1,384,512]{2,1,0:T(8,128)(2,1)S(1)}, bf16[1,384,512]{2,1,0:T(8,128)(2,1)}, u32[]{:S(2)}, u32[]{:S(2)}) %collective-permute-start) | collective-permute-done | bytes 393248 | tf_op jit(solution)/shard_map/ppermute | solution.py:23
  12.4 2.4 %collective-permute-start.7 = (bf16[1,384,512]{2,1,0:T(8,128)(2,1)S(1)}, bf16[1,384,512]{2,1,0:T(8,128)(2,1)S(1)}, u32[]{:S(2)}, u32[]{:S(2)}) collective-permute-start(bf16[1,384,512]{2,1,0:T(8,128)(2,1)S(1)} %get-tuple-element.13), channel_id=1, source_target_pairs={{0,1},{1,0},{2,3},{3,2},{4,5},{5,4},{6,7},{7,6},{8,9},{9,8},{10,11... | collective-permute-start | bytes 1179656 | tf_op jit(solution)/shard_map/ppermute | solution.py:23
  16.6 2.9 %collective-permute-start.1 = (bf16[2,1,384,512]{3,2,1,0:T(8,128)(2,1)S(1)}, bf16[2,1,384,512]{3,2,1,0:T(8,128)(2,1)S(1)}, u32[]{:S(2)}, u32[]{:S(2)}) collective-permute-start(bf16[2,1,384,512]{3,2,1,0:T(8,128)(2,1)S(1)} %stack.8.kn_ref.vn_ref), channel_id=1, source_target_pairs={{0,128},{2,130},{4,132},{6,134},{8,136},{10,138},{12,140},{14,142}... | collective-permute-start | bytes 2359304 | tf_op jit(solution)/shard_map/ppermute | solution.py:19
  19.4 2.7 %collective-permute-start.2 = (bf16[2,1,384,512]{3,2,1,0:T(8,128)(2,1)S(1)}, bf16[2,1,384,512]{3,2,1,0:T(8,128)(2,1)S(1)}, u32[]{:S(2)}, u32[]{:S(2)}) collective-permute-start(bf16[2,1,384,512]{3,2,1,0:T(8,128)(2,1)S(1)} %stack.8.kn_ref.vn_ref), channel_id=1, source_target_pairs={{0,64},{2,66},{4,68},{6,70},{8,72},{10,74},{12,76},{14,78},{16,80}... | collective-permute-start | bytes 2359304 | tf_op jit(solution)/shard_map/ppermute | solution.py:19
  22.5 6.9 %collective-permute-start.4 = (bf16[2,1,384,512]{3,2,1,0:T(8,128)(2,1)S(1)}, bf16[2,1,384,512]{3,2,1,0:T(8,128)(2,1)S(1)}, u32[]{:S(2)}, u32[]{:S(2)}) collective-permute-start(bf16[2,1,384,512]{3,2,1,0:T(8,128)(2,1)S(1)} %stack.8.kn_ref.vn_ref), channel_id=1, source_target_pairs={{0,16},{2,18},{4,20},{6,22},{8,24},{10,26},{12,28},{14,30},{16,0},... | collective-permute-start | bytes 2359304 | tf_op jit(solution)/shard_map/ppermute | solution.py:19
  33.3 8.7 %collective-permute-done.1 = bf16[2,1,384,512]{3,2,1,0:T(8,128)(2,1)S(1)} collective-permute-done((bf16[2,1,384,512]{3,2,1,0:T(8,128)(2,1)S(1)}, bf16[2,1,384,512]{3,2,1,0:T(8,128)(2,1)S(1)}, u32[]{:S(2)}, u32[]{:S(2)}) %collective-permute-start.1) | collective-permute-done | bytes 786464 | tf_op jit(solution)/shard_map/ppermute | solution.py:19
  42.0 2.7 %collective-permute-start.9 = (bf16[2,1,384,512]{3,2,1,0:T(8,128)(2,1)}, bf16[2,1,384,512]{3,2,1,0:T(8,128)(2,1)}, u32[]{:S(2)}, u32[]{:S(2)}) collective-permute-start(bf16[2,1,384,512]{3,2,1,0:T(8,128)(2,1)} %stack.9.kn_ref.vn_ref), channel_id=1, source_target_pairs={{0,64},{2,66},{4,68},{6,70},{8,72},{10,74},{12,76},{14,78},{16,80}... | collective-permute-start | bytes 2359304 | tf_op jit(solution)/shard_map/ppermute | solution.py:19
  45.1 9.9 %collective-permute-done.3 = bf16[2,1,384,512]{3,2,1,0:T(8,128)(2,1)S(1)} collective-permute-done((bf16[2,1,384,512]{3,2,1,0:T(8,128)(2,1)S(1)}, bf16[2,1,384,512]{3,2,1,0:T(8,128)(2,1)S(1)}, u32[]{:S(2)}, u32[]{:S(2)}) %collective-permute-start.3) | collective-permute-done | bytes 786464 | tf_op jit(solution)/shard_map/ppermute | solution.py:19
  55.0 6.9 %collective-permute-start.11 = (bf16[2,1,384,512]{3,2,1,0:T(8,128)(2,1)}, bf16[2,1,384,512]{3,2,1,0:T(8,128)(2,1)}, u32[]{:S(2)}, u32[]{:S(2)}) collective-permute-start(bf16[2,1,384,512]{3,2,1,0:T(8,128)(2,1)} %stack.9.kn_ref.vn_ref), channel_id=1, source_target_pairs={{0,16},{2,18},{4,20},{6,22},{8,24},{10,26},{12,28},{14,30},{16,0},... | collective-permute-start | bytes 2359304 | tf_op jit(solution)/shard_map/ppermute | solution.py:19
  62.8 13.8 %shard_map.73 = bf16[1,384,512]{2,1,0:T(8,128)(2,1)} custom-call(s32[12]{0:T(128)} %reshape.302.off_ref, bf16[1,384,512]{2,1,0:T(8,128)(2,1)} %slice_bitcast_fusion.1.q_ref, bf16[2,1,384,512]{3,2,1,0:T(8,128)(2,1)} %copy-done.1, bf16[2,1,384,512]{3,2,1,0:T(8,128)(2,1)} %copy-done.1, bf16[2,1,3,128,512]{4,3,2,1,0:T(8,128)(2,1)} %bitcast.88, ...), custom_call_target="tpu_custom_call" | custom-call | tf_op jit(solution)/shard_map/pallas_call | solution.py:106
  76.7 2.8 %fusion.26 = bf16[1,384,1024]{2,1,0:T(8,128)(2,1)} fusion(bf16[512,1024]{1,0:T(8,128)(2,1)} %param.11, bf16[1,384,512]{2,1,0:T(8,128)(2,1)} %shard_map.73), kind=kOutput, calls=%fused_computation.42 | convolution fusion | flops 403046400 | bytes 2228224 | tf_op jit(solution)/shard_map/sth,hd->std/dot_general | solution.py:162
  81.3 7.4 %collective-permute-done.10 = bf16[2,1,384,512]{3,2,1,0:T(8,128)(2,1)} collective-permute-done((bf16[2,1,384,512]{3,2,1,0:T(8,128)(2,1)}, bf16[2,1,384,512]{3,2,1,0:T(8,128)(2,1)}, u32[]{:S(2)}, u32[]{:S(2)}) %collective-permute-start.10) | collective-permute-done | bytes 786464 | tf_op jit(solution)/shard_map/ppermute | solution.py:19
  88.7 13.3 %collective-permute-done.11 = bf16[2,1,384,512]{3,2,1,0:T(8,128)(2,1)} collective-permute-done((bf16[2,1,384,512]{3,2,1,0:T(8,128)(2,1)}, bf16[2,1,384,512]{3,2,1,0:T(8,128)(2,1)}, u32[]{:S(2)}, u32[]{:S(2)}) %collective-permute-start.11) | collective-permute-done | bytes 786464 | tf_op jit(solution)/shard_map/ppermute | solution.py:19
  101.9 13.8 %shard_map.74 = bf16[1,384,512]{2,1,0:T(8,128)(2,1)} custom-call(s32[12]{0:T(128)} %reshape.302.off_ref, bf16[1,384,512]{2,1,0:T(8,128)(2,1)} %slice_bitcast_fusion.q_ref, bf16[2,1,384,512]{3,2,1,0:T(8,128)(2,1)} %stack.9.kn_ref.vn_ref, bf16[2,1,384,512]{3,2,1,0:T(8,128)(2,1)} %stack.9.kn_ref.vn_ref, bf16[2,1,3,128,512]{4,3,2,1,0:T(8,128)(2,1)} %bitcast.29.refs_0_.refs_1_, ...), custom_call_target="tpu_custom_call" | custom-call | tf_op jit(solution)/shard_map/pallas_call | solution.py:106
  115.7 2.9 %fusion.27 = bf16[1,384,1024]{2,1,0:T(8,128)(2,1)} fusion(bf16[512,1024]{1,0:T(8,128)(2,1)} %param.11, bf16[1,384,512]{2,1,0:T(8,128)(2,1)} %shard_map.74), kind=kOutput, calls=%fused_computation.43 | convolution fusion | flops 403046400 | bytes 2228224 | tf_op jit(solution)/shard_map/sth,hd->std/dot_general | solution.py:162
  118.6 2.6 %fusion.18 = (f32[384]{0:T(512)S(1)}, bf16[1,384,1024]{2,1,0:T(8,128)(2,1)}) fusion(bf16[1,384,1024]{2,1,0:T(8,128)(2,1)} %collective-permute-done.5, bf16[1,384,1024]{2,1,0:T(8,128)(2,1)} %fusion.26, bf16[1,384,512]{2,1,0:T(8,128)(2,1)S(1)} %copy-done.3, bf16[1,384,512]{2,1,0:T(8,128)(2,1)S(1)} %get-tuple-element.9), kind=kLoop, calls=%fused_computation.28 | loop fusion | flops 4718208 | bytes 3147264 | tf_op jit(solution)/shard_map/reduce_sum | solution.py:122
  121.2 7.1 %fusion.30 = f32[384,1024]{1,0:T(8,128)} fusion(bf16[1536,1024]{1,0:T(8,128)(2,1)} %param.13, bf16[1024,1536]{1,0:T(8,128)(2,1)} %param.12, bf16[1,384,1024]{2,1,0:T(8,128)(2,1)} %get-tuple-element.6, f32[384]{0:T(512)S(1)} %add_rsqrt_fusion.2), kind=kOutput, calls=%fused_computation.45 | convolution fusion | flops 2422407168 | bytes 8652288 | tf_op jit(solution)/shard_map/stf,fd->std/dot_general | solution.py:173
  128.3 1.9 %fusion.76 = bf16[1,384,512]{2,1,0:T(8,128)(2,1)} fusion(f32[384,1024]{1,0:T(8,128)} %fusion.30, s32[]{:T(128)S(6)} %select_n.44), kind=kLoop, calls=%fused_computation.83 | loop fusion | bytes 786436 | tf_op jit(solution)/shard_map/convert_element_type | solution.py:175
  131.7 5.8 %collective-permute-done.12 = bf16[1,384,1024]{2,1,0:T(8,128)(2,1)} collective-permute-done((bf16[1,384,1024]{2,1,0:T(8,128)(2,1)}, bf16[1,384,1024]{2,1,0:T(8,128)(2,1)}, u32[]{:S(2)}, u32[]{:S(2)}) %collective-permute-start.12) | collective-permute-done | bytes 786464 | tf_op jit(solution)/shard_map/ppermute | solution.py:23
  137.5 2.7 %fusion.22 = (f32[384]{0:T(512)S(1)}, bf16[1,384,1024]{2,1,0:T(8,128)(2,1)}) fusion(bf16[1,384,1024]{2,1,0:T(8,128)(2,1)} %collective-permute-done.12, bf16[1,384,1024]{2,1,0:T(8,128)(2,1)} %fusion.27, bf16[1,384,512]{2,1,0:T(8,128)(2,1)} %copy-done.6, bf16[1,384,512]{2,1,0:T(8,128)(2,1)S(1)} %copy-done.5), kind=kLoop, calls=%fused_computation.32 | loop fusion | flops 4718208 | bytes 3147264 | tf_op jit(solution)/shard_map/reduce_sum | solution.py:122
  140.2 7.0 %fusion.28 = f32[384,1024]{1,0:T(8,128)} fusion(bf16[1536,1024]{1,0:T(8,128)(2,1)} %param.13, bf16[1024,1536]{1,0:T(8,128)(2,1)} %param.12, bf16[1,384,1024]{2,1,0:T(8,128)(2,1)} %get-tuple-element.8, f32[384]{0:T(512)S(1)} %add_rsqrt_fusion), kind=kOutput, calls=%fused_computation.44 | convolution fusion | flops 2422407168 | bytes 8652288 | tf_op jit(solution)/shard_map/stf,fd->std/dot_general | solution.py:173
  147.3 1.9 %fusion.77 = bf16[1,384,512]{2,1,0:T(8,128)(2,1)} fusion(f32[384,1024]{1,0:T(8,128)} %fusion.28, s32[]{:T(128)S(6)} %select_n.44), kind=kLoop, calls=%fused_computation.84 | loop fusion | bytes 786436 | tf_op jit(solution)/shard_map/convert_element_type | solution.py:175
  150.9 6.9 %collective-permute-done.13 = bf16[1,384,512]{2,1,0:T(8,128)(2,1)} collective-permute-done((bf16[1,384,512]{2,1,0:T(8,128)(2,1)}, bf16[1,384,512]{2,1,0:T(8,128)(2,1)}, u32[]{:S(2)}, u32[]{:S(2)}) %collective-permute-start.13) | collective-permute-done | bytes 393248 | tf_op jit(solution)/shard_map/ppermute | solution.py:23
  (66 shorter events, 19.2 us)
Async XLA Ops:
  0.0 15.0 %copy-start = (bf16[3,1024,512]{2,1,0:T(8,128)(2,1)S(1)}, bf16[3,1024,512]{2,1,0:T(8,128)(2,1)}, u32[]{:S(2)}) copy-start(bf16[3,1024,512]{2,1,0:T(8,128)(2,1)} %param.10) | copy-start | bytes 9437188
  1.2 9.9 %collective-permute-start = (bf16[1,384,512]{2,1,0:T(8,128)(2,1)S(1)}, bf16[1,384,512]{2,1,0:T(8,128)(2,1)}, u32[]{:S(2)}, u32[]{:S(2)}) collective-permute-start(bf16[1,384,512]{2,1,0:T(8,128)(2,1)S(1)} %slice.28), channel_id=1, source_target_pairs={{0,1},{1,0},{2,3},{3,2},{4,5},{5,4},{6,7},{7,6},{8,9},{9,8},{10,11... | collective-permute-start | bytes 1179656 | tf_op jit(solution)/shard_map/ppermute | solution.py:23
  12.4 17.8 %collective-permute-start.7 = (bf16[1,384,512]{2,1,0:T(8,128)(2,1)S(1)}, bf16[1,384,512]{2,1,0:T(8,128)(2,1)S(1)}, u32[]{:S(2)}, u32[]{:S(2)}) collective-permute-start(bf16[1,384,512]{2,1,0:T(8,128)(2,1)S(1)} %get-tuple-element.13), channel_id=1, source_target_pairs={{0,1},{1,0},{2,3},{3,2},{4,5},{5,4},{6,7},{7,6},{8,9},{9,8},{10,11... | collective-permute-start | bytes 1179656 | tf_op jit(solution)/shard_map/ppermute | solution.py:23
  16.5 13.7 %copy-start.11 = (bf16[2,384,512]{2,1,0:T(8,128)(2,1)S(1)}, bf16[2,384,512]{2,1,0:T(8,128)(2,1)}, u32[]{:S(2)}) copy-start(bf16[2,384,512]{2,1,0:T(8,128)(2,1)} %param.7) | copy-start | bytes 2359300
  16.6 13.9 %copy-start.1 = (bf16[2,1,384,512]{3,2,1,0:T(8,128)(2,1)}, bf16[2,1,384,512]{3,2,1,0:T(8,128)(2,1)S(1)}, u32[]{:S(2)}) copy-start(bf16[2,1,384,512]{3,2,1,0:T(8,128)(2,1)S(1)} %stack.8.kn_ref.vn_ref) | copy-start | bytes 2359300
  16.6 25.5 %collective-permute-start.1 = (bf16[2,1,384,512]{3,2,1,0:T(8,128)(2,1)S(1)}, bf16[2,1,384,512]{3,2,1,0:T(8,128)(2,1)S(1)}, u32[]{:S(2)}, u32[]{:S(2)}) collective-permute-start(bf16[2,1,384,512]{3,2,1,0:T(8,128)(2,1)S(1)} %stack.8.kn_ref.vn_ref), channel_id=1, source_target_pairs={{0,128},{2,130},{4,132},{6,134},{8,136},{10,138},{12,140},{14,142}... | collective-permute-start | bytes 2359304 | tf_op jit(solution)/shard_map/ppermute | solution.py:19
  19.4 25.4 %collective-permute-start.2 = (bf16[2,1,384,512]{3,2,1,0:T(8,128)(2,1)S(1)}, bf16[2,1,384,512]{3,2,1,0:T(8,128)(2,1)S(1)}, u32[]{:S(2)}, u32[]{:S(2)}) collective-permute-start(bf16[2,1,384,512]{3,2,1,0:T(8,128)(2,1)S(1)} %stack.8.kn_ref.vn_ref), channel_id=1, source_target_pairs={{0,64},{2,66},{4,68},{6,70},{8,72},{10,74},{12,76},{14,78},{16,80}... | collective-permute-start | bytes 2359304 | tf_op jit(solution)/shard_map/ppermute | solution.py:19
  22.2 32.8 %collective-permute-start.3 = (bf16[2,1,384,512]{3,2,1,0:T(8,128)(2,1)S(1)}, bf16[2,1,384,512]{3,2,1,0:T(8,128)(2,1)S(1)}, u32[]{:S(2)}, u32[]{:S(2)}) collective-permute-start(bf16[2,1,384,512]{3,2,1,0:T(8,128)(2,1)S(1)} %stack.8.kn_ref.vn_ref), channel_id=1, source_target_pairs={{0,32},{2,34},{4,36},{6,38},{8,40},{10,42},{12,44},{14,46},{16,48}... | collective-permute-start | bytes 2359304 | tf_op jit(solution)/shard_map/ppermute | solution.py:19
  22.5 39.4 %collective-permute-start.4 = (bf16[2,1,384,512]{3,2,1,0:T(8,128)(2,1)S(1)}, bf16[2,1,384,512]{3,2,1,0:T(8,128)(2,1)S(1)}, u32[]{:S(2)}, u32[]{:S(2)}) collective-permute-start(bf16[2,1,384,512]{3,2,1,0:T(8,128)(2,1)S(1)} %stack.8.kn_ref.vn_ref), channel_id=1, source_target_pairs={{0,16},{2,18},{4,20},{6,22},{8,24},{10,26},{12,28},{14,30},{16,0},... | collective-permute-start | bytes 2359304 | tf_op jit(solution)/shard_map/ppermute | solution.py:19
  32.0 29.9 %copy-start.13 = (bf16[3,1,384,512]{3,2,1,0:T(8,128)(2,1)}, bf16[3,1,384,512]{3,2,1,0:T(8,128)(2,1)S(1)}, u32[]{:S(2)}) copy-start(bf16[3,1,384,512]{3,2,1,0:T(8,128)(2,1)S(1)} %fusion.25) | copy-start | bytes 3538948
  33.0 48.3 %collective-permute-start.8 = (bf16[2,1,384,512]{3,2,1,0:T(8,128)(2,1)}, bf16[2,1,384,512]{3,2,1,0:T(8,128)(2,1)}, u32[]{:S(2)}, u32[]{:S(2)}) collective-permute-start(bf16[2,1,384,512]{3,2,1,0:T(8,128)(2,1)} %stack.9.kn_ref.vn_ref), channel_id=1, source_target_pairs={{0,128},{2,130},{4,132},{6,134},{8,136},{10,138},{12,140},{14,142}... | collective-permute-start | bytes 2359304 | tf_op jit(solution)/shard_map/ppermute | solution.py:19
  42.0 19.8 %copy-start.7 = (bf16[2,1,384,512]{3,2,1,0:T(8,128)(2,1)}, bf16[2,1,384,512]{3,2,1,0:T(8,128)(2,1)S(1)}, u32[]{:S(2)}) copy-start(bf16[2,1,384,512]{3,2,1,0:T(8,128)(2,1)S(1)} %collective-permute-done.1) | copy-start | bytes 2359300
  42.0 39.2 %collective-permute-start.9 = (bf16[2,1,384,512]{3,2,1,0:T(8,128)(2,1)}, bf16[2,1,384,512]{3,2,1,0:T(8,128)(2,1)}, u32[]{:S(2)}, u32[]{:S(2)}) collective-permute-start(bf16[2,1,384,512]{3,2,1,0:T(8,128)(2,1)} %stack.9.kn_ref.vn_ref), channel_id=1, source_target_pairs={{0,64},{2,66},{4,68},{6,70},{8,72},{10,74},{12,76},{14,78},{16,80}... | collective-permute-start | bytes 2359304 | tf_op jit(solution)/shard_map/ppermute | solution.py:19
  44.8 17.1 %copy-start.8 = (bf16[2,1,384,512]{3,2,1,0:T(8,128)(2,1)}, bf16[2,1,384,512]{3,2,1,0:T(8,128)(2,1)S(1)}, u32[]{:S(2)}) copy-start(bf16[2,1,384,512]{3,2,1,0:T(8,128)(2,1)S(1)} %collective-permute-done.2) | copy-start | bytes 2359300
  44.8 43.9 %collective-permute-start.10 = (bf16[2,1,384,512]{3,2,1,0:T(8,128)(2,1)}, bf16[2,1,384,512]{3,2,1,0:T(8,128)(2,1)}, u32[]{:S(2)}, u32[]{:S(2)}) collective-permute-start(bf16[2,1,384,512]{3,2,1,0:T(8,128)(2,1)} %stack.9.kn_ref.vn_ref), channel_id=1, source_target_pairs={{0,32},{2,34},{4,36},{6,38},{8,40},{10,42},{12,44},{14,46},{16,48}... | collective-permute-start | bytes 2359304 | tf_op jit(solution)/shard_map/ppermute | solution.py:19
  55.0 6.9 %copy-start.9 = (bf16[2,1,384,512]{3,2,1,0:T(8,128)(2,1)}, bf16[2,1,384,512]{3,2,1,0:T(8,128)(2,1)S(1)}, u32[]{:S(2)}) copy-start(bf16[2,1,384,512]{3,2,1,0:T(8,128)(2,1)S(1)} %collective-permute-done.3) | copy-start | bytes 2359300
  55.0 47.0 %collective-permute-start.11 = (bf16[2,1,384,512]{3,2,1,0:T(8,128)(2,1)}, bf16[2,1,384,512]{3,2,1,0:T(8,128)(2,1)}, u32[]{:S(2)}, u32[]{:S(2)}) collective-permute-start(bf16[2,1,384,512]{3,2,1,0:T(8,128)(2,1)} %stack.9.kn_ref.vn_ref), channel_id=1, source_target_pairs={{0,16},{2,18},{4,20},{6,22},{8,24},{10,26},{12,28},{14,30},{16,0},... | collective-permute-start | bytes 2359304 | tf_op jit(solution)/shard_map/ppermute | solution.py:19
  79.5 39.1 %collective-permute-start.5 = (bf16[1,384,1024]{2,1,0:T(8,128)(2,1)}, bf16[1,384,1024]{2,1,0:T(8,128)(2,1)}, u32[]{:S(2)}, u32[]{:S(2)}) collective-permute-start(bf16[1,384,1024]{2,1,0:T(8,128)(2,1)} %fusion.26), channel_id=1, source_target_pairs={{0,1},{1,0},{2,3},{3,2},{4,5},{5,4},{6,7},{7,6},{8,9},{9,8},{10,11... | collective-permute-start | bytes 2359304 | tf_op jit(solution)/shard_map/ppermute | solution.py:23
  115.7 2.9 %copy-start.3 = (bf16[1,384,512]{2,1,0:T(8,128)(2,1)S(1)}, bf16[1,384,512]{2,1,0:T(8,128)(2,1)}, u32[]{:S(2)}) copy-start(bf16[1,384,512]{2,1,0:T(8,128)(2,1)} %copy-done.2) | copy-start | bytes 1179652
  118.6 18.9 %collective-permute-start.12 = (bf16[1,384,1024]{2,1,0:T(8,128)(2,1)}, bf16[1,384,1024]{2,1,0:T(8,128)(2,1)}, u32[]{:S(2)}, u32[]{:S(2)}) collective-permute-start(bf16[1,384,1024]{2,1,0:T(8,128)(2,1)} %fusion.27), channel_id=1, source_target_pairs={{0,1},{1,0},{2,3},{3,2},{4,5},{5,4},{6,7},{7,6},{8,9},{9,8},{10,11... | collective-permute-start | bytes 2359304 | tf_op jit(solution)/shard_map/ppermute | solution.py:23
  121.2 16.3 %copy-start.5 = (bf16[1,384,512]{2,1,0:T(8,128)(2,1)S(1)}, bf16[1,384,512]{2,1,0:T(8,128)(2,1)}, u32[]{:S(2)}) copy-start(bf16[1,384,512]{2,1,0:T(8,128)(2,1)} %copy-done.4) | copy-start | bytes 1179652
  130.3 19.1 %collective-permute-start.6 = (bf16[1,384,512]{2,1,0:T(8,128)(2,1)}, bf16[1,384,512]{2,1,0:T(8,128)(2,1)}, u32[]{:S(2)}, u32[]{:S(2)}) collective-permute-start(bf16[1,384,512]{2,1,0:T(8,128)(2,1)} %fusion.76), channel_id=1, source_target_pairs={{0,1},{1,0},{2,3},{3,2},{4,5},{5,4},{6,7},{7,6},{8,9},{9,8},{10,11... | collective-permute-start | bytes 1179656 | tf_op jit(solution)/shard_map/ppermute | solution.py:23
  149.2 8.7 %collective-permute-start.13 = (bf16[1,384,512]{2,1,0:T(8,128)(2,1)}, bf16[1,384,512]{2,1,0:T(8,128)(2,1)}, u32[]{:S(2)}, u32[]{:S(2)}) collective-permute-start(bf16[1,384,512]{2,1,0:T(8,128)(2,1)} %fusion.77), channel_id=1, source_target_pairs={{0,1},{1,0},{2,3},{3,2},{4,5},{5,4},{6,7},{7,6},{8,9},{9,8},{10,11... | collective-permute-start | bytes 1179656 | tf_op jit(solution)/shard_map/ppermute | solution.py:23
  149.3 8.5 %copy-start.12 = (bf16[1,384,1024]{2,1,0:T(8,128)(2,1)S(1)}, bf16[1,384,1024]{2,1,0:T(8,128)(2,1)}, u32[]{:S(2)}) copy-start(bf16[1,384,1024]{2,1,0:T(8,128)(2,1)} %get-tuple-element.8) | copy-start | bytes 2359300
  (4 other events, 7.1 us)
